TPU v7x, 256 devices: a whole 4x4x8 slice. The times are simulated.
256 devices in a mesh: tm: 16 (over z, core), pitch: 16 (over y, x).
Axes of the slice: x: 4, y: 4, z: 8, core: 2. Of those that a mesh axis runs over, the one named last changes fastest.
Arguments:
- queries: bfloat16 [128, 512, 2048], P('pitch', 'tm'), may hold values from -30 to 30
- keys: bfloat16 [128, 512, 2048], P('pitch', 'tm'), may hold values from -30 to 30
- values: bfloat16 [128, 512, 2048], P('pitch', 'tm'), may hold values from -6 to 6
- cotangent: bfloat16 [128, 512, 2048], P('pitch', 'tm'), may hold values from -6 to 6
- w_out: bfloat16 [2048, 2048], replicated, may hold values from -0.125 to 0.125
- block_lists: int32 [32, 4], replicated, may hold values from 0 to 31, as said below
- list_counts: int32 [32], replicated, may hold values from 2 to 4, as said below
Outputs:
- block_out: bfloat16 [128, 512, 2048], P('pitch', 'tm')
- grad_queries: bfloat16 [128, 512, 2048], P('pitch', 'tm')
- grad_keys: bfloat16 [128, 512, 2048], P('pitch', 'tm')
- grad_values: bfloat16 [128, 512, 2048], P('pitch', 'tm')
Inputs may be any that keep to these rules, and one draw needn't show every extreme that they name: `block_lists`: entry 0 of row b is b; entries 0 to list_counts[b] - 1 are distinct blocks within 2 blocks of b; later entries equal b. `list_counts`: some block uses all 4 entries.
All inputs are finite; a program needn't handle non-finite values.
Results may differ from a plain program's by a relative error of at most 0.034.
Values may be sent and summed in bfloat16 or wider, within the bound.
No kernel may reach another device: no remote copies, remote signals or barrier semaphores. Data moves between devices by JAX's collectives and lax.ppermute only.
A program may use at most 192 MiB of HBM per device.

v0:
```python
import math

import jax
import jax.numpy as jnp
from jax import lax
from jax.sharding import PartitionSpec as P

E = 128
HT = 8
HP = 8
BT = 16
NL = 4


NEG_FILL = -1e30


def padded(block, sides, width):
    for axis, dim in sides:
        count = lax.axis_size(axis)
        forward = [(i, i + 1) for i in range(count - 1)]
        backward = [(target, source) for source, target in forward]
        low = lax.ppermute(
            lax.slice_in_dim(block, block.shape[dim] - width, None, axis=dim), axis, forward
        )
        high = lax.ppermute(lax.slice_in_dim(block, 0, width, axis=dim), axis, backward)
        block = jnp.concatenate([low, block, high], axis=dim)
    return block


def from_behind(value, axis, by):
    peers = lax.axis_size(axis)
    pairs = [(i, i + by) for i in range(peers) if 0 <= i + by < peers]
    return lax.ppermute(value, axis, pairs)


def time_scores(query_block, key_sel, usable):
    scale = 1.0 / math.sqrt(query_block.shape[-1])
    scores = (
        jnp.einsum("ajihe,ajlkhe->ajhilk", query_block, key_sel, preferred_element_type=jnp.float32)
        * scale
    )
    return jnp.where(usable[None, :, None, None, :, None], scores, NEG_FILL)


def time_forward(query_block, key_sel, value_sel, usable):
    scores = time_scores(query_block, key_sel, usable)
    row_max = jnp.max(scores, axis=(4, 5), keepdims=True)
    expo = jnp.exp(scores - row_max)
    total = jnp.sum(expo, axis=(4, 5), keepdims=True)
    weights = (expo / total).astype(jnp.bfloat16)
    output = jnp.einsum(
        "ajhilk,ajlkhe->ajihe", weights, value_sel, preferred_element_type=jnp.float32
    )
    return (output, row_max + jnp.log(total))


def time_grads(query_block, key_sel, value_sel, usable, grad_block, delta, log_total):
    scores = time_scores(query_block, key_sel, usable)
    back = jnp.exp(scores - log_total)
    dprob = jnp.einsum(
        "ajihe,ajlkhe->ajhilk", grad_block, value_sel, preferred_element_type=jnp.float32
    )
    dscore = (back * (dprob - delta)).astype(jnp.bfloat16)
    return (back.astype(jnp.bfloat16), dscore)


def pitch_stats(query, key):
    scale = 1.0 / math.sqrt(query.shape[-1])
    scores = jnp.einsum("pshe,kshe->shpk", query, key, preferred_element_type=jnp.float32) * scale
    row_max = jnp.max(scores, axis=-1, keepdims=True)
    expo = jnp.exp(scores - row_max)
    total = jnp.sum(expo, axis=-1, keepdims=True)
    return (scores, row_max, expo, total)


def pitch_forward(query, key, value):
    scores, row_max, expo, total = pitch_stats(query, key)
    weights = (expo / total).astype(jnp.bfloat16)
    return jnp.einsum("shpk,kshe->pshe", weights, value, preferred_element_type=jnp.float32)


def pitch_backward(query, key, value, grad, attn):
    scale = 1.0 / math.sqrt(query.shape[-1])
    scores, row_max, expo, total = pitch_stats(query, key)
    back = jnp.exp(scores - (row_max + jnp.log(total)))
    dprob = jnp.einsum("pshe,kshe->shpk", grad, value, preferred_element_type=jnp.float32)
    delta = jnp.einsum("pshe,pshe->shp", grad, attn, preferred_element_type=jnp.float32)[..., None]
    dscore = (back * (dprob - delta)).astype(jnp.bfloat16)
    grad_query = (
        jnp.einsum("shpk,kshe->pshe", dscore, key, preferred_element_type=jnp.float32) * scale
    )
    grad_key = (
        jnp.einsum("shpk,pshe->kshe", dscore, query, preferred_element_type=jnp.float32) * scale
    )
    grad_value = jnp.einsum(
        "shpk,pshe->kshe", back.astype(jnp.bfloat16), grad, preferred_element_type=jnp.float32
    )
    return (
        grad_query.astype(jnp.bfloat16),
        grad_key.astype(jnp.bfloat16),
        grad_value.astype(jnp.bfloat16),
    )


def local(queries, keys, values, cotangent, w_out, block_lists, list_counts):
    rows_pitch, rows_time, width = queries.shape
    spread = rows_time // BT
    time_width = HT * E
    scale = 1.0 / math.sqrt(E)
    my_index = lax.axis_index("tm")
    first_block = my_index * spread
    slot_ids = jnp.arange(NL, dtype=jnp.int32)
    q_time = queries[..., :time_width]
    q_blocks = q_time.reshape(rows_pitch, spread, BT, HT, E)
    kv_own = jnp.stack([keys[..., :time_width], values[..., :time_width]])
    kv_wide = padded(kv_own, (("tm", 2),), rows_time)
    kv_blocks = kv_wide.reshape(2, rows_pitch, 3 * spread, BT, HT, E)
    my_lists = lax.dynamic_slice_in_dim(block_lists, first_block, spread, 0)
    my_counts = lax.dynamic_slice_in_dim(list_counts, first_block, spread, 0)
    usable = slot_ids[None, :] < my_counts[:, None]
    local_ids = (my_lists - first_block + spread).reshape(-1)
    key_sel = jnp.take(kv_blocks[0], local_ids, axis=1).reshape(rows_pitch, spread, NL, BT, HT, E)
    value_sel = jnp.take(kv_blocks[1], local_ids, axis=1).reshape(rows_pitch, spread, NL, BT, HT, E)
    time_out, time_log = time_forward(q_blocks, key_sel, value_sel, usable)
    q_pitch = queries[..., time_width:].reshape(rows_pitch, rows_time, HP, E)
    k_pitch = keys[..., time_width:].reshape(rows_pitch, rows_time, HP, E)
    v_pitch = values[..., time_width:].reshape(rows_pitch, rows_time, HP, E)
    exchanged = (
        lax.all_to_all(q_pitch, "pitch", split_axis=1, concat_axis=0, tiled=True),
        lax.all_to_all(k_pitch, "pitch", split_axis=1, concat_axis=0, tiled=True),
        lax.all_to_all(v_pitch, "pitch", split_axis=1, concat_axis=0, tiled=True),
    )
    local_out = pitch_forward(exchanged[0], exchanged[1], exchanged[2]).astype(jnp.bfloat16)
    pitch_out = lax.all_to_all(local_out, "pitch", split_axis=0, concat_axis=1, tiled=True)
    attention = jnp.concatenate(
        [
            time_out.reshape(rows_pitch, rows_time, time_width).astype(jnp.bfloat16),
            pitch_out.reshape(rows_pitch, rows_time, HP * E),
        ],
        axis=-1,
    )
    flat = attention.reshape(rows_pitch * rows_time, width)
    block_out = (
        jnp.dot(flat, w_out, preferred_element_type=jnp.float32)
        .astype(jnp.bfloat16)
        .reshape(queries.shape)
    )
    d_attention = lax.dot_general(
        cotangent.reshape(rows_pitch * rows_time, width),
        w_out,
        (((1,), (1,)), ((), ())),
        preferred_element_type=jnp.float32,
    )
    d_attention = d_attention.astype(jnp.bfloat16).reshape(queries.shape)
    d_pitch = d_attention[..., time_width:].reshape(rows_pitch, rows_time, HP, E)
    a_pitch = attention[..., time_width:].reshape(rows_pitch, rows_time, HP, E)
    exchanged = (
        lax.all_to_all(q_pitch, "pitch", split_axis=1, concat_axis=0, tiled=True),
        lax.all_to_all(k_pitch, "pitch", split_axis=1, concat_axis=0, tiled=True),
        lax.all_to_all(v_pitch, "pitch", split_axis=1, concat_axis=0, tiled=True),
        lax.all_to_all(d_pitch, "pitch", split_axis=1, concat_axis=0, tiled=True),
        lax.all_to_all(a_pitch, "pitch", split_axis=1, concat_axis=0, tiled=True),
    )
    local_grads = pitch_backward(
        exchanged[0], exchanged[1], exchanged[2], exchanged[3], exchanged[4]
    )
    d_time_rows = d_attention[..., :time_width]
    d_blocks = d_time_rows.reshape(rows_pitch, spread, BT, HT, E)
    a_blocks = attention[..., :time_width].reshape(rows_pitch, spread, BT, HT, E)
    delta_rows = jnp.sum(d_blocks.astype(jnp.float32) * a_blocks.astype(jnp.float32), axis=-1)
    delta_time = jnp.transpose(delta_rows, (0, 1, 3, 2))[..., None, None]
    back_half, dscore = time_grads(
        q_blocks, key_sel, value_sel, usable, d_blocks, delta_time, time_log
    )
    grad_query_time = (
        jnp.einsum("ajhilk,ajlkhe->ajihe", dscore, key_sel, preferred_element_type=jnp.float32)
        * scale
    )
    key_terms = (
        jnp.einsum("ajhilk,ajihe->ajlkhe", dscore, q_blocks, preferred_element_type=jnp.float32)
        * scale
    )
    value_terms = jnp.einsum(
        "ajhilk,ajihe->ajlkhe", back_half, d_blocks, preferred_element_type=jnp.float32
    )
    onehot = (
        local_ids.reshape(spread, NL)[:, :, None]
        == jnp.arange(3 * spread, dtype=jnp.int32)[None, None, :]
    ).astype(jnp.float32)
    wide_grads = jnp.einsum(
        "jlc,xajlkhe->xackhe",
        onehot,
        jnp.stack([key_terms, value_terms]),
        precision=lax.Precision.HIGHEST,
    )
    from_left = from_behind(wide_grads[:, :, 2 * spread :].astype(jnp.bfloat16), "tm", 1).astype(
        jnp.float32
    )
    from_right = from_behind(wide_grads[:, :, :spread].astype(jnp.bfloat16), "tm", -1).astype(
        jnp.float32
    )
    key_grads = wide_grads[:, :, spread : 2 * spread] + from_left + from_right
    pitch_width = HP * E
    grad_queries = jnp.concatenate(
        [
            grad_query_time.reshape(rows_pitch, rows_time, time_width).astype(jnp.bfloat16),
            lax.all_to_all(
                local_grads[0], "pitch", split_axis=0, concat_axis=1, tiled=True
            ).reshape(rows_pitch, rows_time, pitch_width),
        ],
        axis=-1,
    )
    grad_keys = jnp.concatenate(
        [
            key_grads[0].reshape(rows_pitch, rows_time, time_width).astype(jnp.bfloat16),
            lax.all_to_all(
                local_grads[1], "pitch", split_axis=0, concat_axis=1, tiled=True
            ).reshape(rows_pitch, rows_time, pitch_width),
        ],
        axis=-1,
    )
    grad_values = jnp.concatenate(
        [
            key_grads[1].reshape(rows_pitch, rows_time, time_width).astype(jnp.bfloat16),
            lax.all_to_all(
                local_grads[2], "pitch", split_axis=0, concat_axis=1, tiled=True
            ).reshape(rows_pitch, rows_time, pitch_width),
        ],
        axis=-1,
    )
    return (block_out, grad_queries, grad_keys, grad_values)


def solution(mesh):
    return jax.shard_map(
        local,
        mesh=mesh,
        in_specs=(
            P("pitch", "tm", None),
            P("pitch", "tm", None),
            P("pitch", "tm", None),
            P("pitch", "tm", None),
            P(),
            P(),
            P(),
        ),
        out_specs=(
            P("pitch", "tm", None),
            P("pitch", "tm", None),
            P("pitch", "tm", None),
            P("pitch", "tm", None),
        ),
        check_vma=False,
    )
```

profile of v0, /device:TPU:65, one launch (start us, length us, event | category | flops | bytes accessed | tf_op | source)
XLA Modules:
  0.0 201.1 jit_solution(15877397543684588588)
XLA Ops:
  0.6 2.2 %fusion.87 = (bf16[8,32,1024]{2,1,0:T(8,128)(2,1)}, bf16[8,32,1024]{2,1,0:T(8,128)(2,1)S(1)}) fusion(bf16[8,32,2048]{2,1,0:T(8,128)(2,1)} %param.9), kind=kLoop, calls=%fused_computation.113 | loop fusion | bytes 2097152 | tf_op jit(solution)/shard_map/slice | solution.py:114
  3.9 6.8 %all-to-all-start = ((bf16[8,32,8,128]{3,2,0,1:T(8,128)(2,1)}), bf16[8,32,8,128]{3,2,0,1:T(8,128)(2,1)S(1)}, u32[]{:S(2)}, u32[]{:S(2)}) async-start(bf16[8,32,8,128]{3,2,0,1:T(8,128)(2,1)} %copy.233), calls=%async_computation | async-start | bytes 1048576 | tf_op jit(solution)/shard_map/all_to_all | solution.py:130
  10.6 1.7 slice_bitcast_fusion
  13.5 2.9 %collective-permute-start.1 = (bf16[2,8,32,1024]{3,2,1,0:T(8,128)(2,1)}, bf16[2,8,32,1024]{3,2,1,0:T(8,128)(2,1)}, u32[]{:S(2)}, u32[]{:S(2)}) collective-permute-start(bf16[2,8,32,1024]{3,2,1,0:T(8,128)(2,1)} %pad_maximum_fusion.2), channel_id=1, source_target_pairs={{16,0},{32,16},{48,32},{64,48},{80,64},{96,80},{112,96},{128,112},... | collective-permute-start | bytes 3145736 | tf_op jit(solution)/shard_map/ppermute | solution.py:26
  16.4 3.4 %collective-permute-start = (bf16[2,8,32,1024]{3,2,1,0:T(8,128)(2,1)}, bf16[2,8,32,1024]{3,2,1,0:T(8,128)(2,1)}, u32[]{:S(2)}, u32[]{:S(2)}) collective-permute-start(bf16[2,8,32,1024]{3,2,1,0:T(8,128)(2,1)} %pad_maximum_fusion.2), channel_id=1, source_target_pairs={{0,16},{16,32},{32,48},{48,64},{64,80},{80,96},{96,112},{112,128},... | collective-permute-start | bytes 3145736 | tf_op jit(solution)/shard_map/ppermute | solution.py:23
  21.1 6.8 %all-to-all-start.1 = ((bf16[8,32,8,128]{3,2,0,1:T(8,128)(2,1)}), bf16[8,32,8,128]{3,2,0,1:T(8,128)(2,1)S(1)}, u32[]{:S(2)}, u32[]{:S(2)}) async-start(bf16[8,32,8,128]{3,2,0,1:T(8,128)(2,1)} %copy.235), calls=%async_computation.1 | async-start | bytes 1048576 | tf_op jit(solution)/shard_map/all_to_all | solution.py:131
  27.8 6.7 %convolution_convert_fusion = bf16[256,2048]{1,0:T(8,128)(2,1)} fusion(bf16[256,2048]{1,0:T(8,128)(2,1)S(1)} %bitcast.220, bf16[2048,2048]{1,0:T(8,128)(2,1)} %param.13), kind=kOutput, calls=%fused_computation.18 | convolution fusion | flops 2148007936 | bytes 10485760 | tf_op jit(solution)/shard_map/dot_general | solution.py:149
  35.6 2.1 %fusion.86 = (bf16[8,32,1024]{2,1,0:T(8,128)(2,1)}, bf16[8,32,1024]{2,1,0:T(8,128)(2,1)S(1)}) fusion(bf16[8,32,2048]{2,1,0:T(8,128)(2,1)} %bitcast.262), kind=kLoop, calls=%fused_computation.112 | loop fusion | bytes 2097152 | tf_op jit(solution)/shard_map/slice | solution.py:168
  37.7 1.7 all-to-all-done.1
  39.3 5.0 %all-to-all-start.2 = ((bf16[8,32,8,128]{3,2,0,1:T(8,128)(2,1)}), bf16[8,32,8,128]{3,2,0,1:T(8,128)(2,1)S(1)}, u32[]{:S(2)}, u32[]{:S(2)}) async-start(bf16[8,32,8,128]{3,2,0,1:T(8,128)(2,1)} %copy.237), calls=%async_computation.2 | async-start | bytes 1048576 | tf_op jit(solution)/shard_map/all_to_all | solution.py:132
  45.7 10.5 %all-to-all-done.2 = bf16[8,32,8,128]{3,2,0,1:T(8,128)(2,1)S(1)} async-done(((bf16[8,32,8,128]{3,2,0,1:T(8,128)(2,1)}), bf16[8,32,8,128]{3,2,0,1:T(8,128)(2,1)S(1)}, u32[]{:S(2)}, u32[]{:S(2)}) %all-to-all-start.2) | async-done | bytes 524320 | tf_op jit(solution)/shard_map/all_to_all | solution.py:132
  56.2 3.6 %all-to-all-start.4 = ((bf16[8,32,8,128]{3,2,0,1:T(8,128)(2,1)}), bf16[8,32,8,128]{3,2,0,1:T(8,128)(2,1)S(1)}, u32[]{:S(2)}, u32[]{:S(2)}) async-start(bf16[8,32,8,128]{3,2,0,1:T(8,128)(2,1)} %copy.243), calls=%async_computation.4 | async-start | bytes 1048576 | tf_op jit(solution)/shard_map/all_to_all | solution.py:162
  60.4 1.5 fusion.39
  63.1 7.4 %all-to-all-done.4 = bf16[8,32,8,128]{3,2,0,1:T(8,128)(2,1)S(1)} async-done(((bf16[8,32,8,128]{3,2,0,1:T(8,128)(2,1)}), bf16[8,32,8,128]{3,2,0,1:T(8,128)(2,1)S(1)}, u32[]{:S(2)}, u32[]{:S(2)}) %all-to-all-start.4) | async-done | bytes 524320 | tf_op jit(solution)/shard_map/all_to_all | solution.py:162
  70.4 3.6 %all-to-all-start.3 = ((bf16[128,2,8,128]{3,2,1,0:T(8,128)(2,1)}), bf16[128,2,8,128]{3,2,1,0:T(8,128)(2,1)S(1)}, u32[]{:S(2)}, u32[]{:S(2)}) async-start(bf16[128,2,8,128]{3,2,1,0:T(8,128)(2,1)} %copy.171), calls=%async_computation.3 | async-start | bytes 1048576 | tf_op jit(solution)/shard_map/all_to_all | solution.py:135
  74.0 1.3 fusion.40
  75.4 2.2 %copy.203 = bf16[128,2,8,128]{3,2,1,0:T(8,128)(2,1)} copy(bf16[128,2,8,128]{0,3,2,1:T(8,128)(2,1)} %fusion.40) | data formatting | bytes 1048576 | tf_op jit(solution)/shard_map/convert_element_type | solution.py:102
  77.6 6.5 %all-to-all-done.3 = bf16[128,2,8,128]{3,2,1,0:T(8,128)(2,1)S(1)} async-done(((bf16[128,2,8,128]{3,2,1,0:T(8,128)(2,1)}), bf16[128,2,8,128]{3,2,1,0:T(8,128)(2,1)S(1)}, u32[]{:S(2)}, u32[]{:S(2)}) %all-to-all-start.3) | async-done | bytes 524320 | tf_op jit(solution)/shard_map/all_to_all | solution.py:135
  84.1 4.2 %all-to-all-start.8 = ((bf16[128,2,8,128]{3,2,1,0:T(8,128)(2,1)}), bf16[128,2,8,128]{3,2,1,0:T(8,128)(2,1)}, u32[]{:S(2)}, u32[]{:S(2)}) async-start(bf16[128,2,8,128]{3,2,1,0:T(8,128)(2,1)} %copy.203), calls=%async_computation.8 | async-start | bytes 1048576 | tf_op jit(solution)/shard_map/all_to_all | solution.py:226
  88.4 1.9 copy.256
  94.3 3.3 %all-to-all-done.8 = bf16[128,2,8,128]{3,2,1,0:T(8,128)(2,1)} async-done(((bf16[128,2,8,128]{3,2,1,0:T(8,128)(2,1)}), bf16[128,2,8,128]{3,2,1,0:T(8,128)(2,1)}, u32[]{:S(2)}, u32[]{:S(2)}) %all-to-all-start.8) | async-done | bytes 524320 | tf_op jit(solution)/shard_map/all_to_all | solution.py:226
  97.6 4.4 %all-to-all-start.5 = ((bf16[8,32,8,128]{3,2,0,1:T(8,128)(2,1)}), bf16[8,32,8,128]{3,2,0,1:T(8,128)(2,1)}, u32[]{:S(2)}, u32[]{:S(2)}) async-start(bf16[8,32,8,128]{3,2,0,1:T(8,128)(2,1)} %copy.184), calls=%async_computation.5 | async-start | bytes 1048576 | tf_op jit(solution)/shard_map/all_to_all | solution.py:163
  104.2 1.7 pad_maximum_fusion.1
  106.8 1.6 copy.249
  108.4 3.6 %gather_fusion.1 = bf16[8,8,16,8,128]{4,3,2,1,0:T(8,128)(2,1)} fusion(bf16[8,6,16,8,128]{4,3,2,1,0:T(8,128)(2,1)} %bitcast.223, s32[1024]{0:T(1024)S(1)} %pad_clamp_fusion), kind=kCustom, calls=%fused_computation.1.clone | custom fusion | bytes 4194336 | tf_op jit(solution)/shard_map/jit(_take)/gather | solution.py:123
  111.9 2.1 %gather_fusion = bf16[8,8,16,8,128]{4,3,2,1,0:T(8,128)(2,1)} fusion(bf16[8,6,16,8,128]{4,3,2,1,0:T(8,128)(2,1)S(1)} %bitcast.222, s32[1024]{0:T(1024)S(1)} %pad_clamp_fusion), kind=kCustom, calls=%fused_computation.clone | custom fusion | bytes 4194336 | tf_op jit(solution)/shard_map/jit(_take)/gather | solution.py:124
  114.1 2.7 %broadcast_select_fusion.1 = (bf16[8,8,16,8,128]{4,3,2,1,0:T(8,128)(2,1)S(1)}, bf16[8,8,16,8,128]{4,3,2,1,0:T(8,128)(2,1)S(1)}) fusion(bf16[8,8,16,8,128]{4,3,2,1,0:T(8,128)(2,1)} %gather_fusion, pred[8]{0:T(512)(128)(4,1)S(1)} %compare_and_fusion, bf16[8,8,16,8,128]{4,3,2,1,0:T(8,128)(2,1)} %gather_fusion.1), kind=kLoop, calls=%fused_computation.24 | loop fusion | flops 2097152 | bytes 8388616 | tf_op jit(solution)/shard_map/jit(_take)/select_n | solution.py:124
  117.8 1.5 fusion.5
  120.5 2.2 %multiply_reduce_fusion.1 = (f32[8,2,16,8]{2,3,1,0:T(8,128)S(1)}, bf16[8,2,16,8,128]{4,2,3,1,0:T(8,128)(2,1)}) fusion(bf16[8,2,16,8,128]{4,3,2,1,0:T(8,128)(2,1)S(1)} %bitcast.257, f32[8,2,8,4,16,16]{5,4,3,2,1,0:T(8,128)S(1)} %get-tuple-element.24, f32[8,2,8,16]{3,2,1,0:T(8,128)S(1)} %fusion.5, f32[8,2,8,16]{3,2,1,0:T(8,128)S(1)} %get-tuple-element.23, ...), kind=kOutput, calls=%fused_computation.62 | convolution fusion | flops 35518464 | bytes 3694600 | tf_op jit(solution)/shard_map/ajhilk,ajlkhe->ajihe/dot_general | solution.py:52
  123.4 1.5 multiply_convert_fusion
  126.2 1.7 pad_maximum_fusion
  127.9 9.9 %fusion.89 = (bf16[2,8,6,16,8,128]{5,2,4,3,1,0:T(8,128)(2,1)S(1)}, f32[2,8,6,16,8,128]{5,2,4,3,1,0:T(8,128)}) fusion(s32[2,4]{1,0:T(2,128)S(1)} %copy.153, f32[2,8,2,4,16,8,128]{6,4,3,5,2,1,0:T(8,128)S(1)} %pad_maximum_fusion), kind=kOutput, calls=%fused_computation.115 | convolution fusion | flops 152567856 | bytes 17825824 | tf_op jit(solution)/shard_map/jlc,xajlkhe->xackhe/dot_general | solution.py:191
  137.8 2.9 %fusion.83 = (bf16[2,8,2,16,8,128]{5,2,4,3,1,0:T(2,128)(2,1)}, bf16[2,8,2,16,8,128]{5,2,4,3,1,0:T(2,128)(2,1)}) fusion(bf16[2,8,6,16,8,128]{5,2,4,3,1,0:T(8,128)(2,1)S(1)} %get-tuple-element.27), kind=kLoop, calls=%fused_computation.109 | loop fusion | bytes 4194304 | tf_op jit(solution)/shard_map/slice | solution.py:197
  141.8 2.0 multiply_reduce_fusion
  144.9 1.2 copy.198
  146.1 6.4 %all-to-all-start.7 = ((bf16[128,2,8,128]{3,2,1,0:T(8,128)(2,1)}), bf16[128,2,8,128]{3,2,1,0:T(8,128)(2,1)S(1)}, u32[]{:S(2)}, u32[]{:S(2)}) async-start(bf16[128,2,8,128]{3,2,1,0:T(8,128)(2,1)} %copy.198), calls=%async_computation.7 | async-start | bytes 1048576 | tf_op jit(solution)/shard_map/all_to_all | solution.py:217
  152.4 3.0 %fusion.41 = bf16[8,2,16,8,128]{4,2,3,1,0:T(8,128)(2,1)S(1)} fusion(bf16[8,2,8,16,4,16]{3,5,4,2,1,0:T(8,128)(2,1)} %copy-done.2, bf16[8,2,4,16,8,128]{5,4,3,0,2,1:T(8,128)(2,1)} %bitcast.229), kind=kOutput, calls=%fused_computation.51 | convolution fusion | flops 34078720 | bytes 2883584 | tf_op jit(solution)/shard_map/ajhilk,ajlkhe->ajihe/dot_general | solution.py:177
  155.8 1.2 copy.160
  157.1 9.4 %collective-permute-start.2 = (bf16[2,8,2,16,8,128]{5,2,4,3,1,0:T(2,128)(2,1)}, bf16[2,8,2,16,8,128]{5,2,4,3,1,0:T(2,128)(2,1)}, u32[]{:S(2)}, u32[]{:S(2)}) collective-permute-start(bf16[2,8,2,16,8,128]{5,2,4,3,1,0:T(2,128)(2,1)} %get-tuple-element.5), channel_id=1, source_target_pairs={{0,16},{16,32},{32,48},{48,64},{64,80},{80,96},{96,112},{112,128},... | collective-permute-start | bytes 3145736 | tf_op jit(solution)/shard_map/ppermute | solution.py:34
  166.5 1.9 collective-permute-start.3
  168.8 1.2 copy.190
  170.0 6.9 %all-to-all-start.6 = ((bf16[128,2,8,128]{3,2,1,0:T(8,128)(2,1)}), bf16[128,2,8,128]{3,2,1,0:T(8,128)(2,1)S(1)}, u32[]{:S(2)}, u32[]{:S(2)}) async-start(bf16[128,2,8,128]{3,2,1,0:T(8,128)(2,1)} %copy.190), calls=%async_computation.6 | async-start | bytes 1048576 | tf_op jit(solution)/shard_map/all_to_all | solution.py:208
  176.9 6.9 %convolution_convert_fusion.1 = bf16[256,2048]{1,0:T(8,128)(2,1)} fusion(bf16[2048,2048]{1,0:T(8,128)(2,1)} %param.13, bf16[256,1024]{1,0:T(8,128)(2,1)} %bitcast.263, bf16[256,1024]{1,0:T(8,128)(2,1)S(1)} %bitcast.264), kind=kOutput, calls=%fused_computation.19 | convolution fusion | flops 2150105088 | bytes 10485760 | tf_op jit(solution)/shard_map/dot_general | solution.py:145
  184.1 3.4 %all-to-all-done.6 = bf16[128,2,8,128]{3,2,1,0:T(8,128)(2,1)S(1)} async-done(((bf16[128,2,8,128]{3,2,1,0:T(8,128)(2,1)}), bf16[128,2,8,128]{3,2,1,0:T(8,128)(2,1)S(1)}, u32[]{:S(2)}, u32[]{:S(2)}) %all-to-all-start.6) | async-done | bytes 524320 | tf_op jit(solution)/shard_map/all_to_all | solution.py:208
  188.9 5.0 %fusion.10 = bf16[2,8,2,16,8,128]{5,2,4,3,1,0:T(2,128)(2,1)S(1)} fusion(f32[2,8,6,16,8,128]{5,2,4,3,1,0:T(8,128)} %get-tuple-element.28, bf16[2,8,2,16,8,128]{5,2,4,3,1,0:T(2,128)(2,1)} %collective-permute-done.3, bf16[2,8,2,16,8,128]{5,2,4,3,1,0:T(2,128)(2,1)} %collective-permute-done.2), kind=kLoop, calls=%fused_computation.22 | loop fusion | flops 2621440 | bytes 5242880 | tf_op jit(solution)/shard_map/convert.2
  193.9 1.5 fusion.85
  195.8 1.1 copy.196
  199.0 2.1 %pad_maximum_fusion.4 = bf16[8,32,2048]{2,1,0:T(8,128)(2,1)} fusion(bf16[8,32,1024]{2,1,0:T(8,128)(2,1)S(1)} %reshape.137, bf16[8,32,1024]{2,1,0:T(8,128)(2,1)} %convert_element_type.114), kind=kLoop, calls=%fused_computation.58 | loop fusion | flops 2097152 | bytes 2097152 | tf_op jit(solution)/shard_map/concatenate | solution.py:214
  (95 shorter events, 25.8 us)
Async XLA Ops:
  0.6 27.2 %copy-start = (bf16[8,32,2048]{2,1,0:T(8,128)(2,1)S(1)}, bf16[8,32,2048]{2,1,0:T(8,128)(2,1)}, u32[]{:S(2)}) copy-start(bf16[8,32,2048]{2,1,0:T(8,128)(2,1)} %param.12) | copy-start | bytes 3145732
  3.9 17.2 %all-to-all-start = ((bf16[8,32,8,128]{3,2,0,1:T(8,128)(2,1)}), bf16[8,32,8,128]{3,2,0,1:T(8,128)(2,1)S(1)}, u32[]{:S(2)}, u32[]{:S(2)}) async-start(bf16[8,32,8,128]{3,2,0,1:T(8,128)(2,1)} %copy.233), calls=%async_computation | async-start | bytes 1048576 | tf_op jit(solution)/shard_map/all_to_all | solution.py:130
  12.4 7.6 %copy-start.8 = (bf16[1,8,32,1024]{3,2,1,0:T(8,128)(2,1)}, bf16[1,8,32,1024]{3,2,1,0:T(8,128)(2,1)S(1)}, u32[]{:S(2)}) copy-start(bf16[1,8,32,1024]{3,2,1,0:T(8,128)(2,1)S(1)} %get-tuple-element.30) | copy-start | bytes 1572868
  13.5 90.7 %collective-permute-start.1 = (bf16[2,8,32,1024]{3,2,1,0:T(8,128)(2,1)}, bf16[2,8,32,1024]{3,2,1,0:T(8,128)(2,1)}, u32[]{:S(2)}, u32[]{:S(2)}) collective-permute-start(bf16[2,8,32,1024]{3,2,1,0:T(8,128)(2,1)} %pad_maximum_fusion.2), channel_id=1, source_target_pairs={{16,0},{32,16},{48,32},{64,48},{80,64},{96,80},{112,96},{128,112},... | collective-permute-start | bytes 3145736 | tf_op jit(solution)/shard_map/ppermute | solution.py:26
  16.4 87.8 %collective-permute-start = (bf16[2,8,32,1024]{3,2,1,0:T(8,128)(2,1)}, bf16[2,8,32,1024]{3,2,1,0:T(8,128)(2,1)}, u32[]{:S(2)}, u32[]{:S(2)}) collective-permute-start(bf16[2,8,32,1024]{3,2,1,0:T(8,128)(2,1)} %pad_maximum_fusion.2), channel_id=1, source_target_pairs={{0,16},{16,32},{32,48},{48,64},{64,80},{80,96},{96,112},{112,128},... | collective-permute-start | bytes 3145736 | tf_op jit(solution)/shard_map/ppermute | solution.py:23
  21.1 38.7 %copy-start.6 = (bf16[8,32,8,128]{3,2,0,1:T(8,128)(2,1)}, bf16[8,32,8,128]{3,2,0,1:T(8,128)(2,1)S(1)}, u32[]{:S(2)}) copy-start(bf16[8,32,8,128]{3,2,0,1:T(8,128)(2,1)S(1)} %all-to-all-done) | copy-start | bytes 1572868
  21.1 18.3 %all-to-all-start.1 = ((bf16[8,32,8,128]{3,2,0,1:T(8,128)(2,1)}), bf16[8,32,8,128]{3,2,0,1:T(8,128)(2,1)S(1)}, u32[]{:S(2)}, u32[]{:S(2)}) async-start(bf16[8,32,8,128]{3,2,0,1:T(8,128)(2,1)} %copy.235), calls=%async_computation.1 | async-start | bytes 1048576 | tf_op jit(solution)/shard_map/all_to_all | solution.py:131
  34.5 9.8 %copy-start.16 = (s32[32,4]{0,1:T(4,128)S(1)}, s32[32,4]{0,1:T(4,128)}, u32[]{:S(2)}) copy-start(s32[32,4]{0,1:T(4,128)} %param.14) | copy-start | bytes 1540
  39.3 22.6 %copy-start.4 = (bf16[8,32,8,128]{3,2,0,1:T(8,128)(2,1)}, bf16[8,32,8,128]{3,2,0,1:T(8,128)(2,1)S(1)}, u32[]{:S(2)}) copy-start(bf16[8,32,8,128]{3,2,0,1:T(8,128)(2,1)S(1)} %all-to-all-done.1) | copy-start | bytes 1572868
  39.3 16.8 %all-to-all-start.2 = ((bf16[8,32,8,128]{3,2,0,1:T(8,128)(2,1)}), bf16[8,32,8,128]{3,2,0,1:T(8,128)(2,1)S(1)}, u32[]{:S(2)}, u32[]{:S(2)}) async-start(bf16[8,32,8,128]{3,2,0,1:T(8,128)(2,1)} %copy.237), calls=%async_computation.2 | async-start | bytes 1048576 | tf_op jit(solution)/shard_map/all_to_all | solution.py:132
  56.2 3.6 %copy-start.10 = (bf16[8,32,8,128]{3,2,0,1:T(8,128)(2,1)}, bf16[8,32,8,128]{3,2,0,1:T(8,128)(2,1)S(1)}, u32[]{:S(2)}) copy-start(bf16[8,32,8,128]{3,2,0,1:T(8,128)(2,1)S(1)} %all-to-all-done.2) | copy-start | bytes 1572868
  56.2 14.3 %all-to-all-start.4 = ((bf16[8,32,8,128]{3,2,0,1:T(8,128)(2,1)}), bf16[8,32,8,128]{3,2,0,1:T(8,128)(2,1)S(1)}, u32[]{:S(2)}, u32[]{:S(2)}) async-start(bf16[8,32,8,128]{3,2,0,1:T(8,128)(2,1)} %copy.243), calls=%async_computation.4 | async-start | bytes 1048576 | tf_op jit(solution)/shard_map/all_to_all | solution.py:162
  61.9 26.4 %copy-start.17 = (s32[32]{0:T(128)S(1)}, s32[32]{0:T(128)}, u32[]{:S(2)}) copy-start(s32[32]{0:T(128)} %param.15) | copy-start | bytes 388
  63.1 27.3 %copy-start.13 = (bf16[8,32,1024]{2,1,0:T(8,128)(2,1)S(1)}, bf16[8,32,1024]{2,1,0:T(8,128)(2,1)}, u32[]{:S(2)}) copy-start(bf16[8,32,1024]{2,1,0:T(8,128)(2,1)} %get-tuple-element.13) | copy-start | bytes 1572868
  70.4 13.6 %all-to-all-start.3 = ((bf16[128,2,8,128]{3,2,1,0:T(8,128)(2,1)}), bf16[128,2,8,128]{3,2,1,0:T(8,128)(2,1)S(1)}, u32[]{:S(2)}, u32[]{:S(2)}) async-start(bf16[128,2,8,128]{3,2,1,0:T(8,128)(2,1)} %copy.171), calls=%async_computation.3 | async-start | bytes 1048576 | tf_op jit(solution)/shard_map/all_to_all | solution.py:135
  84.1 13.6 %all-to-all-start.8 = ((bf16[128,2,8,128]{3,2,1,0:T(8,128)(2,1)}), bf16[128,2,8,128]{3,2,1,0:T(8,128)(2,1)}, u32[]{:S(2)}, u32[]{:S(2)}) async-start(bf16[128,2,8,128]{3,2,1,0:T(8,128)(2,1)} %copy.203), calls=%async_computation.8 | async-start | bytes 1048576 | tf_op jit(solution)/shard_map/all_to_all | solution.py:226
  91.2 12.9 %copy-start.9 = (bf16[1,8,32,1024]{3,2,1,0:T(8,128)(2,1)S(1)}, bf16[1,8,32,1024]{3,2,1,0:T(8,128)(2,1)}, u32[]{:S(2)}) copy-start(bf16[1,8,32,1024]{3,2,1,0:T(8,128)(2,1)} %copy-done.8) | copy-start | bytes 1572868
  97.6 43.0 %all-to-all-start.5 = ((bf16[8,32,8,128]{3,2,0,1:T(8,128)(2,1)}), bf16[8,32,8,128]{3,2,0,1:T(8,128)(2,1)}, u32[]{:S(2)}, u32[]{:S(2)}) async-start(bf16[8,32,8,128]{3,2,0,1:T(8,128)(2,1)} %copy.184), calls=%async_computation.5 | async-start | bytes 1048576 | tf_op jit(solution)/shard_map/all_to_all | solution.py:163
  114.1 2.7 %copy-start.14 = (bf16[32,8,8,128]{3,2,1,0:T(8,128)(2,1)S(1)}, bf16[32,8,8,128]{3,2,1,0:T(8,128)(2,1)}, u32[]{:S(2)}) copy-start(bf16[32,8,8,128]{3,2,1,0:T(8,128)(2,1)} %copy.250) | copy-start | bytes 1572868
  116.8 2.5 %copy-start.3 = (bf16[8,8,16,8,128]{4,3,2,1,0:T(8,128)(2,1)}, bf16[8,8,16,8,128]{4,3,2,1,0:T(8,128)(2,1)S(1)}, u32[]{:S(2)}) copy-start(bf16[8,8,16,8,128]{4,3,2,1,0:T(8,128)(2,1)S(1)} %get-tuple-element.20) | copy-start | bytes 6291460
  119.3 1.2 copy-start.15
  124.8 1.4 copy-start.2
  137.7 6.1 %copy-start.11 = (bf16[8,32,8,128]{3,2,0,1:T(8,128)(2,1)S(1)}, bf16[8,32,8,128]{3,2,0,1:T(8,128)(2,1)}, u32[]{:S(2)}) copy-start(bf16[8,32,8,128]{3,2,0,1:T(8,128)(2,1)} %copy-done.10) | copy-start | bytes 1572868
  137.8 6.6 %copy-start.7 = (bf16[8,32,8,128]{3,2,0,1:T(8,128)(2,1)S(1)}, bf16[8,32,8,128]{3,2,0,1:T(8,128)(2,1)}, u32[]{:S(2)}) copy-start(bf16[8,32,8,128]{3,2,0,1:T(8,128)(2,1)} %copy-done.6) | copy-start | bytes 1572868
  146.1 23.9 %all-to-all-start.7 = ((bf16[128,2,8,128]{3,2,1,0:T(8,128)(2,1)}), bf16[128,2,8,128]{3,2,1,0:T(8,128)(2,1)S(1)}, u32[]{:S(2)}, u32[]{:S(2)}) async-start(bf16[128,2,8,128]{3,2,1,0:T(8,128)(2,1)} %copy.198), calls=%async_computation.7 | async-start | bytes 1048576 | tf_op jit(solution)/shard_map/all_to_all | solution.py:217
  152.4 16.0 %copy-start.5 = (bf16[8,32,8,128]{3,2,0,1:T(8,128)(2,1)S(1)}, bf16[8,32,8,128]{3,2,0,1:T(8,128)(2,1)}, u32[]{:S(2)}) copy-start(bf16[8,32,8,128]{3,2,0,1:T(8,128)(2,1)} %copy-done.4) | copy-start | bytes 1572868
  157.1 31.7 %collective-permute-start.2 = (bf16[2,8,2,16,8,128]{5,2,4,3,1,0:T(2,128)(2,1)}, bf16[2,8,2,16,8,128]{5,2,4,3,1,0:T(2,128)(2,1)}, u32[]{:S(2)}, u32[]{:S(2)}) collective-permute-start(bf16[2,8,2,16,8,128]{5,2,4,3,1,0:T(2,128)(2,1)} %get-tuple-element.5), channel_id=1, source_target_pairs={{0,16},{16,32},{32,48},{48,64},{64,80},{80,96},{96,112},{112,128},... | collective-permute-start | bytes 3145736 | tf_op jit(solution)/shard_map/ppermute | solution.py:34
  166.5 22.4 %collective-permute-start.3 = (bf16[2,8,2,16,8,128]{5,2,4,3,1,0:T(2,128)(2,1)}, bf16[2,8,2,16,8,128]{5,2,4,3,1,0:T(2,128)(2,1)}, u32[]{:S(2)}, u32[]{:S(2)}) collective-permute-start(bf16[2,8,2,16,8,128]{5,2,4,3,1,0:T(2,128)(2,1)} %get-tuple-element.6), channel_id=1, source_target_pairs={{16,0},{32,16},{48,32},{64,48},{80,64},{96,80},{112,96},{128,112},... | collective-permute-start | bytes 3145736 | tf_op jit(solution)/shard_map/ppermute | solution.py:34
  170.0 17.5 %all-to-all-start.6 = ((bf16[128,2,8,128]{3,2,1,0:T(8,128)(2,1)}), bf16[128,2,8,128]{3,2,1,0:T(8,128)(2,1)S(1)}, u32[]{:S(2)}, u32[]{:S(2)}) async-start(bf16[128,2,8,128]{3,2,1,0:T(8,128)(2,1)} %copy.190), calls=%async_computation.6 | async-start | bytes 1048576 | tf_op jit(solution)/shard_map/all_to_all | solution.py:208
  193.9 4.0 %copy-start.12 = (bf16[8,32,1024]{2,1,0:T(8,128)(2,1)S(1)}, bf16[8,32,1024]{2,1,0:T(8,128)(2,1)}, u32[]{:S(2)}) copy-start(bf16[8,32,1024]{2,1,0:T(8,128)(2,1)} %reshape.138) | copy-start | bytes 1572868
  195.4 5.7 %copy-start.1 = (bf16[8,32,2048]{2,1,0:T(8,128)(2,1)S(1)}, bf16[8,32,2048]{2,1,0:T(8,128)(2,1)}, u32[]{:S(2)}) copy-start(bf16[8,32,2048]{2,1,0:T(8,128)(2,1)} %param.12) | copy-start | bytes 3145732
where the time goes:
time: 203 us; the launch traced here: 201 us
  starting transfers between devices  65.2 us (32%)
  local copies, waits for them, and re-layouts  42.1 us (21%)
  matrix products  37.2 us (18%)
  waiting for transfers between devices  32.9 us (16%)
  other arithmetic  22.5 us (11%)
    ppermute x2, starting transfers between devices, from_behind(): return lax.ppermute(value, axis, pairs)  11.3 us
    all_to_all x1, waiting for transfers between devices, local(): lax.all_to_all(v_pitch, 'pitch', split_axis=1, concat_axis=0, tiled=True)  10.5 us
    dot_general x1, matrix products, local(): jnp.einsum('jlc,xajlkhe->xackhe', onehot, jnp.stack([key_terms, value_ter...  9.88 us
    all_to_all x1, waiting for transfers between devices, local(): lax.all_to_all(d_pitch, 'pitch', split_axis=1, concat_axis=0, tiled=True)  7.36 us
    unnamed x46, local copies, waits for them, and re-layouts  6.97 us
    all_to_all x1, starting transfers between devices, local(): lax.all_to_all(local_grads[0], 'pitch', split_axis=0, concat_axis=1, tile...  6.94 us
    dot_general x1, matrix products, local(): jnp.dot(flat, w_out, preferred_element_type=jnp.float32)  6.87 us
    all_to_all x1, starting transfers between devices, local(): lax.all_to_all(q_pitch, 'pitch', split_axis=1, concat_axis=0, tiled=True)  6.75 us
  transfers between devices with their start and end apart: 13, of which 7 were waited for; matrix products, arithmetic and copies ran while one was open for 40% of the time, Pallas kernels for 0%

commit v1 on v0

v1 whole, which is shorter than its diff:
```python
import math

import jax
import jax.numpy as jnp
from jax import lax
from jax.sharding import PartitionSpec as P

E = 128
HT = 8
HP = 8
BT = 16
NL = 4


NEG_FILL = -1e30


def shift(value, axis, by):
    peers = lax.axis_size(axis)
    pairs = [(i, i + by) for i in range(peers) if 0 <= i + by < peers]
    return lax.ppermute(value, axis, pairs)


def attend(query, key, value, grad, mask, scale, qspec, kspec):
    sspec = "bhqk"
    f32 = jnp.float32
    scores = jnp.einsum(f"{qspec},{kspec}->{sspec}", query, key, preferred_element_type=f32)
    scores = scores * scale
    if mask is not None:
        scores = jnp.where(mask, scores, NEG_FILL)
    row_max = jnp.max(scores, axis=-1, keepdims=True)
    expo = jnp.exp(scores - row_max)
    total = jnp.sum(expo, axis=-1, keepdims=True)
    weights = (expo / total).astype(jnp.bfloat16)
    out = jnp.einsum(f"{sspec},{kspec}->{qspec}", weights, value, preferred_element_type=f32)
    out16 = out.astype(jnp.bfloat16)
    log_total = row_max + jnp.log(total)
    back = jnp.exp(scores - log_total)
    dprob = jnp.einsum(f"{qspec},{kspec}->{sspec}", grad, value, preferred_element_type=f32)
    delta = jnp.einsum(f"{qspec},{qspec}->bhq", grad, out16, preferred_element_type=f32)
    dscore = (back * (dprob - delta[..., None])).astype(jnp.bfloat16)
    grad_query = jnp.einsum(f"{sspec},{kspec}->{qspec}", dscore, key, preferred_element_type=f32)
    grad_key = jnp.einsum(f"{sspec},{qspec}->{kspec}", dscore, query, preferred_element_type=f32)
    grad_value = jnp.einsum(
        f"{sspec},{qspec}->{kspec}", back.astype(jnp.bfloat16), grad, preferred_element_type=f32
    )
    return out16, grad_query * scale, grad_key * scale, grad_value


def local(queries, keys, values, cotangent, w_out, block_lists, list_counts):
    rows_pitch, rows_time, width = queries.shape
    spread = rows_time // BT
    time_width = HT * E
    scale = 1.0 / math.sqrt(E)
    bf16 = jnp.bfloat16

    d_attention = lax.dot_general(
        cotangent.reshape(rows_pitch * rows_time, width),
        w_out,
        (((1,), (1,)), ((), ())),
        preferred_element_type=jnp.float32,
    )
    d_attention = d_attention.astype(bf16).reshape(queries.shape)

    def pitch_part(x):
        return x[..., time_width:].reshape(rows_pitch, rows_time, HP, E)

    sent = jnp.stack([pitch_part(queries), pitch_part(keys), pitch_part(values), pitch_part(d_attention)])
    got = lax.all_to_all(sent, "pitch", split_axis=2, concat_axis=1, tiled=True)
    p_out, p_gq, p_gk, p_gv = attend(
        got[0], got[1], got[2], got[3], None, scale, "qbhe", "kbhe"
    )
    back = jnp.stack([p_out, p_gq.astype(bf16), p_gk.astype(bf16), p_gv.astype(bf16)])
    returned = lax.all_to_all(back, "pitch", split_axis=1, concat_axis=2, tiled=True)
    returned = returned.reshape(4, rows_pitch, rows_time, HP * E)

    me = lax.axis_index("tm")
    first_block = me * spread
    kv_own = jnp.stack([keys[..., :time_width], values[..., :time_width]])
    kv_wide = jnp.concatenate([shift(kv_own, "tm", 1), kv_own, shift(kv_own, "tm", -1)], axis=2)
    my_lists = lax.dynamic_slice_in_dim(block_lists, first_block, spread, 0)
    my_counts = lax.dynamic_slice_in_dim(list_counts, first_block, spread, 0)
    used = jnp.arange(NL, dtype=jnp.int32)[None, :] < my_counts[:, None]
    slots = first_block - spread + jnp.arange(3 * spread, dtype=jnp.int32)
    allowed = jnp.any(used[:, :, None] & (my_lists[:, :, None] == slots[None, None, :]), axis=1)
    mask = jnp.repeat(jnp.repeat(allowed, BT, axis=0), BT, axis=1)[None, None]

    def heads(x):
        return x.reshape(x.shape[0], x.shape[1], HT, E)

    t_out, t_gq, t_gk, t_gv = attend(
        heads(queries[..., :time_width]),
        heads(kv_wide[0]),
        heads(kv_wide[1]),
        heads(d_attention[..., :time_width]),
        mask,
        scale,
        "bqhe",
        "bkhe",
    )
    g_wide = jnp.stack([t_gk, t_gv]).reshape(2, rows_pitch, 3 * rows_time, time_width)
    from_next = shift(g_wide[:, :, :rows_time].astype(bf16), "tm", -1)
    from_prev = shift(g_wide[:, :, 2 * rows_time :].astype(bf16), "tm", 1)
    g_own = (
        g_wide[:, :, rows_time : 2 * rows_time]
        + from_next.astype(jnp.float32)
        + from_prev.astype(jnp.float32)
    )

    attention = jnp.concatenate([t_out.reshape(rows_pitch, rows_time, time_width), returned[0]], axis=-1)
    block_out = (
        jnp.dot(attention.reshape(rows_pitch * rows_time, width), w_out, preferred_element_type=jnp.float32)
        .astype(bf16)
        .reshape(queries.shape)
    )
    grad_queries = jnp.concatenate(
        [t_gq.reshape(rows_pitch, rows_time, time_width).astype(bf16), returned[1]], axis=-1
    )
    grad_keys = jnp.concatenate([g_own[0].astype(bf16), returned[2]], axis=-1)
    grad_values = jnp.concatenate([g_own[1].astype(bf16), returned[3]], axis=-1)
    return (block_out, grad_queries, grad_keys, grad_values)


def solution(mesh):
    return jax.shard_map(
        local,
        mesh=mesh,
        in_specs=(
            P("pitch", "tm", None),
            P("pitch", "tm", None),
            P("pitch", "tm", None),
            P("pitch", "tm", None),
            P(),
            P(),
            P(),
        ),
        out_specs=(
            P("pitch", "tm", None),
            P("pitch", "tm", None),
            P("pitch", "tm", None),
            P("pitch", "tm", None),
        ),
        check_vma=False,
    )
```

time: 203 us -> 129 us (0.64)
  starting transfers between devices: 65.2 us -> 25.6 us
  matrix products: 37.2 us -> 24.3 us
  other arithmetic: 22.5 us -> 11.2 us
  waiting for transfers between devices: 32.9 us -> 24 us
    all_to_all x9 -> x2, starting transfers between devices: 47.6 us -> 13.6 us  [the longest x1 6.95 us: local(): got = lax.all_to_all(sent, 'pitch', split_axis=2, concat_axis=1, tiled=True)]
    all_to_all x9 -> x2, waiting for transfers between devices: 32.9 us -> 14.3 us  [the longest x1 14.3 us: local(): lax.all_to_all(back, 'pitch', split_axis=1, concat_axis=2, tiled=True)]
    another operation x0 -> x5, local copies, waits for them, and re-layouts: none -> 12.4 us  [the longest x3 7.63 us: local(): jnp.stack([t_gk, t_gv]).reshape(2, rows_pitch, 3 * rows_time, time_width)]
    dot_general x13, matrix products: 29.8 us -> 18.6 us  [the longest x1 6.68 us: local(): jnp.dot(attention.reshape(rows_pitch * rows_time, width), w_out, preferre...]
    ppermute x4, waiting for transfers between devices: 0.01 us -> 9.65 us  [shift(): return lax.ppermute(value, axis, pairs)]
    convert_element_type x9 -> x3, local copies, waits for them, and re-layouts: 8.55 us -> 0.42 us  [the longest x1 0.21 us: attend(): out16 = out.astype(jnp.bfloat16)]
    slice x7 -> x5, local copies, waits for them, and re-layouts: 10.3 us -> 2.45 us  [the longest x1 1.33 us: local(): grad_values = jnp.concatenate([g_own[1].astype(bf16), returned[3]], axis=-1)]
    gather x2 -> x0, local copies, waits for them, and re-layouts: 5.71 us -> none  [the longest x1 3.58 us: local(): jnp.take(kv_blocks[0], local_ids, axis=1)]
  transfers between devices with their start and end apart: 13 -> 6, of which waited for: 7 -> 3; matrix products, arithmetic and copies ran while one was open for 40% -> 35% of each run, Pallas kernels for 0% -> 0%
where the time goes in v1:
time: 129 us
  local copies, waits for them, and re-layouts  42.4 us (33%)
  starting transfers between devices  25.6 us (20%)
  matrix products  24.3 us (19%)
  waiting for transfers between devices  24 us (19%)
  other arithmetic  11.2 us (9%)
    all_to_all x1, waiting for transfers between devices, local(): lax.all_to_all(back, 'pitch', split_axis=1, concat_axis=2, tiled=True)  14.3 us
    ppermute x4, starting transfers between devices, shift(): return lax.ppermute(value, axis, pairs)  12 us
    unnamed x50, local copies, waits for them, and re-layouts  11.8 us
    ppermute x4, waiting for transfers between devices, shift(): return lax.ppermute(value, axis, pairs)  9.65 us
    another operation x3, local copies, waits for them, and re-layouts, local(): jnp.stack([t_gk, t_gv]).reshape(2, rows_pitch, 3 * rows_time, time_width)  7.63 us
    all_to_all x1, starting transfers between devices, local(): got = lax.all_to_all(sent, 'pitch', split_axis=2, concat_axis=1, tiled=True)  6.95 us
    dot_general x1, matrix products, local(): jnp.dot(attention.reshape(rows_pitch * rows_time, width), w_out, preferre...  6.68 us
    all_to_all x1, starting transfers between devices, local(): lax.all_to_all(back, 'pitch', split_axis=1, concat_axis=2, tiled=True)  6.64 us
  transfers between devices with their start and end apart: 6, of which 3 were waited for; matrix products, arithmetic and copies ran while one was open for 35% of the time, Pallas kernels for 0%

profile of v1, /device:TPU:65, one launch (start us, length us, event | category | flops | bytes accessed | tf_op | source)
XLA Modules:
  0.0 128.6 jit_solution(990083537060948559)
XLA Ops:
  0.6 1.8 %slice_bitcast_fusion.3 = (bf16[1,8,32,1024]{3,2,1,0:T(8,128)(2,1)S(1)}, bf16[8,32,1024]{2,1,0:T(8,128)(2,1)S(1)}, bf16[8,32,1024]{2,1,0:T(8,128)(2,1)S(1)}, bf16[1,8,32,1024]{3,2,1,0:T(8,128)(2,1)S(1)}) fusion(bf16[8,32,2048]{2,1,0:T(8,128)(2,1)} %param.9, bf16[8,32,2048]{2,1,0:T(8,128)(2,1)} %param.8), kind=kLoop, calls=%fused_computation.86 | loop fusion | bytes 4194304 | tf_op jit(solution)/shard_map/stack | solution.py:79
  2.5 1.1 pad_maximum_fusion.3
  3.6 2.6 %collective-permute-start.1 = (bf16[2,8,32,1024]{3,2,1,0:T(8,128)(2,1)}, bf16[2,8,32,1024]{3,2,1,0:T(8,128)(2,1)}, u32[]{:S(2)}, u32[]{:S(2)}) collective-permute-start(bf16[2,8,32,1024]{3,2,1,0:T(8,128)(2,1)} %pad_maximum_fusion.3), channel_id=1, source_target_pairs={{16,0},{32,16},{48,32},{64,48},{80,64},{96,80},{112,96},{128,112},... | collective-permute-start | bytes 3145736 | tf_op jit(solution)/shard_map/ppermute | solution.py:21
  6.1 3.4 %collective-permute-start = (bf16[2,8,32,1024]{3,2,1,0:T(8,128)(2,1)}, bf16[2,8,32,1024]{3,2,1,0:T(8,128)(2,1)}, u32[]{:S(2)}, u32[]{:S(2)}) collective-permute-start(bf16[2,8,32,1024]{3,2,1,0:T(8,128)(2,1)} %pad_maximum_fusion.3), channel_id=1, source_target_pairs={{0,16},{16,32},{32,48},{48,64},{64,80},{80,96},{96,112},{112,128},... | collective-permute-start | bytes 3145736 | tf_op jit(solution)/shard_map/ppermute | solution.py:21
  9.6 5.7 %convolution_convert_fusion.1 = bf16[256,2048]{1,0:T(8,128)(2,1)S(1)} fusion(bf16[256,2048]{1,0:T(8,128)(2,1)S(1)} %bitcast.161, bf16[2048,2048]{1,0:T(8,128)(2,1)} %param.11), kind=kOutput, calls=%fused_computation.3 | convolution fusion | flops 2148007936 | bytes 10485760 | tf_op jit(solution)/shard_map/dot_general | solution.py:57
  15.7 0.9 copy-done.14
  17.4 2.0 %copy.202 = bf16[4,8,32,8,128]{4,3,1,0,2:T(8,128)(2,1)} copy(bf16[4,8,32,8,128]{4,3,2,1,0:T(8,128)(2,1)S(1)} %pad_maximum_fusion.1) | data formatting | bytes 4194304 | tf_op jit(solution)/shard_map/stack | solution.py:68
  19.4 6.9 %all-to-all-start = ((bf16[4,8,32,8,128]{4,3,1,0,2:T(8,128)(2,1)}), bf16[4,8,32,8,128]{4,3,1,0,2:T(8,128)(2,1)}, u32[]{:S(2)}, u32[]{:S(2)}) async-start(bf16[4,8,32,8,128]{4,3,1,0,2:T(8,128)(2,1)} %copy.202), calls=%async_computation | async-start | bytes 4194304 | tf_op jit(solution)/shard_map/all_to_all | solution.py:69
  27.3 1.0 fusion.57
  28.3 1.7 %pad_maximum_fusion = bf16[2,8,96,1024]{3,2,1,0:T(8,128)(2,1)S(1)} fusion(bf16[2,8,32,1024]{3,2,1,0:T(8,128)(2,1)} %collective-permute-done.1, bf16[1,8,32,1024]{3,2,1,0:T(8,128)(2,1)S(1)} %get-tuple-element.25, bf16[1,8,32,1024]{3,2,1,0:T(8,128)(2,1)S(1)} %get-tuple-element.36, bf16[2,8,32,1024]{3,2,1,0:T(8,128)(2,1)} %collective-permute-done), kind=kLoop, calls=%fused_computation | loop fusion | flops 12582912 | bytes 6291456 | tf_op jit(solution)/shard_map/concatenate | solution.py:80
  30.9 1.6 %copy.208 = bf16[96,8,8,128]{3,2,1,0:T(8,128)(2,1)} copy(bf16[96,8,8,128]{3,1,2,0:T(8,128)(2,1)S(1)} %bitcast.168) | data formatting | bytes 3145728
  32.5 1.0 fusion.92
  33.6 0.7 fusion.51
  34.5 1.3 %convolution_bitcast_fusion = f32[8,96,8,128]{3,1,2,0:T(8,128)S(1)} fusion(f32[8,8,32,96]{3,2,1,0:T(8,128)S(1)} %get-tuple-element.32, f32[8,8,32]{2,1,0:T(8,128)S(1)} %log_add_fusion, bf16[8,4,8,8,128]{4,3,2,1,0:T(8,128)(2,1)S(1)} %get-tuple-element.18), kind=kOutput, calls=%fused_computation.10 | convolution fusion | flops 50724864 | bytes 4464640 | tf_op jit(solution)/shard_map/bhqk,bqhe->bkhe/dot_general | solution.py:44
  35.9 3.4 %copy.173 = f32[8,96,8,128]{3,2,1,0:T(8,128)} copy(f32[8,96,8,128]{3,1,2,0:T(8,128)S(1)} %convolution_bitcast_fusion) | data formatting | bytes 6291456 | tf_op jit(solution)/shard_map/bhqk,bqhe->bkhe/transpose | solution.py:44
  39.3 2.8 %stack.46 = f32[1,8,96,1024]{3,2,1,0:T(8,128)S(1)} reshape(f32[8,96,8,128]{3,2,1,0:T(8,128)} %copy.173) | data formatting | bytes 6291456 | tf_op jit(solution)/shard_map/stack | solution.py:101
  42.2 3.7 %multiply_reduce_fusion = (f32[8,8,32]{2,1,0:T(8,128)S(1)}, bf16[8,8,128,32]{2,3,1,0:T(8,128)(2,1)}) fusion(f32[8,8,32,128]{3,1,2,0:T(8,128)} %fusion.57, bf16[8,96,8,128]{3,2,1,0:T(8,128)(2,1)} %bitcast.166, f32[8,8,32,96]{3,2,1,0:T(8,128)} %copy-done.3, f32[8,8,32]{2,1,0:T(8,128)S(1)} %fusion.51, f32[8,8,32]{2,1,0:T(8,128)S(1)} %get-tuple-element.31), kind=kOutput, calls=%fused_computation.51 | convolution fusion | flops 51968000 | bytes 3956736 | tf_op jit(solution)/shard_map/bhqk,bkhe->bqhe/dot_general | solution.py:35
  45.9 1.1 fusion.35
  47.0 0.8 copy-done.10
  47.8 0.6 multiply_bitcast_fusion
  48.4 3.4 %copy.171 = f32[8,96,8,128]{3,2,1,0:T(8,128)} copy(f32[8,96,8,128]{3,1,2,0:T(8,128)S(1)} %multiply_bitcast_fusion) | data formatting | bytes 6291456 | tf_op jit(solution)/shard_map/mul | solution.py:47
  51.8 4.6 %stack.45 = f32[1,8,96,1024]{3,2,1,0:T(8,128)} reshape(f32[8,96,8,128]{3,2,1,0:T(8,128)} %copy.171) | data formatting | bytes 6291456 | tf_op jit(solution)/shard_map/stack | solution.py:101
  56.4 2.1 %constant_dynamic-update-slice_fusion.1 = f32[2,8,96,1024]{3,2,1,0:T(8,128)S(1)} fusion(f32[1,8,96,1024]{3,2,1,0:T(8,128)} %stack.45), kind=kLoop, calls=%fused_computation.103 | loop fusion | bytes 6291456
  58.8 2.6 %copy-done.2 = f32[2,8,96,1024]{3,2,1,0:T(8,128)} copy-done((f32[2,8,96,1024]{3,2,1,0:T(8,128)}, f32[2,8,96,1024]{3,2,1,0:T(8,128)S(1)}, u32[]{:S(2)}) %copy-start.2) | copy-done | bytes 6291480
  61.9 2.1 %copy.145 = bf16[4,8,32,8,128]{4,3,2,1,0:T(8,128)(2,1)S(1)} copy(bf16[4,8,32,8,128]{4,3,1,0,2:T(8,128)(2,1)} %all-to-all-done) | data formatting | bytes 4194304 | tf_op jit(solution)/shard_map/all_to_all | solution.py:69
  64.6 0.8 fusion.91
  65.6 0.8 fusion.50
  66.3 0.5 fusion.46
  66.8 0.6 fusion.29
  67.9 0.5 fusion.42
  68.7 2.7 %copy.164 = bf16[4,128,2,8,128]{4,3,2,0,1:T(8,128)(2,1)} copy(bf16[4,128,2,8,128]{4,1,3,2,0:T(8,128)(2,1)S(1)} %pad_maximum_fusion.2) | data formatting | bytes 4194304 | tf_op jit(solution)/shard_map/stack | solution.py:73
  71.5 6.6 %all-to-all-start.1 = ((bf16[4,128,2,8,128]{4,3,2,0,1:T(8,128)(2,1)}), bf16[4,128,2,8,128]{4,3,2,0,1:T(8,128)(2,1)}, u32[]{:S(2)}, u32[]{:S(2)}) async-start(bf16[4,128,2,8,128]{4,3,2,0,1:T(8,128)(2,1)} %copy.164), calls=%async_computation.1 | async-start | bytes 4194304 | tf_op jit(solution)/shard_map/all_to_all | solution.py:74
  78.3 2.1 %collective-permute-start.2 = (bf16[2,8,32,1024]{3,2,1,0:T(8,128)(2,1)S(1)}, bf16[2,8,32,1024]{3,2,1,0:T(8,128)(2,1)S(1)}, u32[]{:S(2)}, u32[]{:S(2)}) collective-permute-start(bf16[2,8,32,1024]{3,2,1,0:T(8,128)(2,1)S(1)} %get-tuple-element.4), channel_id=1, source_target_pairs={{16,0},{32,16},{48,32},{64,48},{80,64},{96,80},{112,96},{128,112},... | collective-permute-start | bytes 3145736 | tf_op jit(solution)/shard_map/ppermute | solution.py:21
  80.4 3.9 %collective-permute-start.3 = (bf16[2,8,32,1024]{3,2,1,0:T(8,128)(2,1)S(1)}, bf16[2,8,32,1024]{3,2,1,0:T(8,128)(2,1)S(1)}, u32[]{:S(2)}, u32[]{:S(2)}) collective-permute-start(bf16[2,8,32,1024]{3,2,1,0:T(8,128)(2,1)S(1)} %get-tuple-element.5), channel_id=1, source_target_pairs={{0,16},{16,32},{32,48},{48,64},{64,80},{80,96},{96,112},{112,128},... | collective-permute-start | bytes 3145736 | tf_op jit(solution)/shard_map/ppermute | solution.py:21
  84.3 0.5 fusion.43
  85.2 0.9 copy.308
  86.1 8.9 %collective-permute-done.2 = bf16[2,8,32,1024]{3,2,1,0:T(8,128)(2,1)S(1)} collective-permute-done((bf16[2,8,32,1024]{3,2,1,0:T(8,128)(2,1)S(1)}, bf16[2,8,32,1024]{3,2,1,0:T(8,128)(2,1)S(1)}, u32[]{:S(2)}, u32[]{:S(2)}) %collective-permute-start.2) | collective-permute-done | bytes 1048608 | tf_op jit(solution)/shard_map/ppermute | solution.py:21
  95.0 0.8 collective-permute-done.3
  95.7 2.2 %fusion.1 = bf16[2,8,32,1024]{3,2,1,0:T(8,128)(2,1)S(1)} fusion(f32[2,8,96,1024]{3,2,1,0:T(8,128)} %copy-done.2, bf16[2,8,32,1024]{3,2,1,0:T(8,128)(2,1)S(1)} %collective-permute-done.3, bf16[2,8,32,1024]{3,2,1,0:T(8,128)(2,1)S(1)} %collective-permute-done.2), kind=kLoop, calls=%fused_computation.6 | loop fusion | flops 2621440 | bytes 5242880 | tf_op jit(solution)/shard_map/convert.1
  98.0 14.3 %all-to-all-done.1 = bf16[4,128,2,8,128]{4,3,2,0,1:T(8,128)(2,1)} async-done(((bf16[4,128,2,8,128]{4,3,2,0,1:T(8,128)(2,1)}), bf16[4,128,2,8,128]{4,3,2,0,1:T(8,128)(2,1)}, u32[]{:S(2)}, u32[]{:S(2)}) %all-to-all-start.1) | async-done | bytes 2097184 | tf_op jit(solution)/shard_map/all_to_all | solution.py:74
  112.3 2.2 %copy.306 = bf16[4,16,8,2,8,128]{5,4,3,1,2,0:T(8,128)(2,1)S(1)} copy(bf16[4,16,8,2,8,128]{5,4,3,0,2,1:T(8,128)(2,1)} %bitcast.28) | data formatting | bytes 4194304 | tf_op jit(solution)/shard_map/all_to_all | solution.py:74
  114.5 1.3 %fusion.89 = (bf16[1,8,16,2,8,128]{5,4,3,2,1,0:T(8,128)(2,1)S(1)}, bf16[1,8,16,2,8,128]{5,4,3,2,1,0:T(8,128)(2,1)S(1)}, bf16[1,8,16,2,8,128]{5,4,3,2,1,0:T(8,128)(2,1)}, bf16[1,8,16,2,8,128]{5,4,3,2,1,0:T(8,128)(2,1)}) fusion(bf16[4,8,16,2,8,128]{5,4,3,2,1,0:T(8,128)(2,1)S(1)} %bitcast.163), kind=kLoop, calls=%fused_computation.112 | loop fusion | bytes 4194304 | tf_op jit(solution)/shard_map/slice | solution.py:120
  116.3 1.3 squeeze.28
  117.6 1.2 copy.307
  118.8 1.1 pad_maximum_fusion.4
  119.8 6.7 %convolution_convert_fusion = bf16[256,2048]{1,0:T(8,128)(2,1)} fusion(bf16[2048,2048]{1,0:T(8,128)(2,1)} %param.11, bf16[256,1024]{1,0:T(8,128)(2,1)S(1)} %bitcast.188, bf16[256,1024]{1,0:T(8,128)(2,1)S(1)} %bitcast.187), kind=kOutput, calls=%fused_computation.2 | convolution fusion | flops 2150105088 | bytes 10485760 | tf_op jit(solution)/shard_map/dot_general | solution.py:112
  126.5 1.1 pad_maximum_fusion.6
  127.6 1.1 pad_maximum_fusion.5
  (74 shorter events, 6.3 us)
Async XLA Ops:
  0.6 9.0 %copy-start = (bf16[8,32,2048]{2,1,0:T(8,128)(2,1)S(1)}, bf16[8,32,2048]{2,1,0:T(8,128)(2,1)}, u32[]{:S(2)}) copy-start(bf16[8,32,2048]{2,1,0:T(8,128)(2,1)} %param.10) | copy-start | bytes 3145732
  3.6 24.7 %collective-permute-start.1 = (bf16[2,8,32,1024]{3,2,1,0:T(8,128)(2,1)}, bf16[2,8,32,1024]{3,2,1,0:T(8,128)(2,1)}, u32[]{:S(2)}, u32[]{:S(2)}) collective-permute-start(bf16[2,8,32,1024]{3,2,1,0:T(8,128)(2,1)} %pad_maximum_fusion.3), channel_id=1, source_target_pairs={{16,0},{32,16},{48,32},{64,48},{80,64},{96,80},{112,96},{128,112},... | collective-permute-start | bytes 3145736 | tf_op jit(solution)/shard_map/ppermute | solution.py:21
  6.1 22.2 %collective-permute-start = (bf16[2,8,32,1024]{3,2,1,0:T(8,128)(2,1)}, bf16[2,8,32,1024]{3,2,1,0:T(8,128)(2,1)}, u32[]{:S(2)}, u32[]{:S(2)}) collective-permute-start(bf16[2,8,32,1024]{3,2,1,0:T(8,128)(2,1)} %pad_maximum_fusion.3), channel_id=1, source_target_pairs={{0,16},{16,32},{32,48},{48,64},{64,80},{80,96},{96,112},{112,128},... | collective-permute-start | bytes 3145736 | tf_op jit(solution)/shard_map/ppermute | solution.py:21
  15.4 1.2 copy-start.14
  16.6 17.7 %copy-start.8 = (bf16[8,4,8,8,128]{4,3,2,1,0:T(8,128)(2,1)}, bf16[8,4,8,8,128]{4,3,2,1,0:T(8,128)(2,1)S(1)}, u32[]{:S(2)}) copy-start(bf16[8,4,8,8,128]{4,3,2,1,0:T(8,128)(2,1)S(1)} %get-tuple-element.18) | copy-start | bytes 1572868
  16.7 15.8 %copy-start.12 = (bf16[8,4,8,8,128]{4,3,2,1,0:T(8,128)(2,1)}, bf16[8,4,8,8,128]{4,3,2,1,0:T(8,128)(2,1)S(1)}, u32[]{:S(2)}) copy-start(bf16[8,4,8,8,128]{4,3,2,1,0:T(8,128)(2,1)S(1)} %get-tuple-element.21) | copy-start | bytes 1572868
  19.4 7.0 %copy-start.18 = (s32[32]{0:T(128)S(1)}, s32[32]{0:T(128)}, u32[]{:S(2)}) copy-start(s32[32]{0:T(128)} %param.13) | copy-start | bytes 388
  19.4 7.1 %copy-start.17 = (s32[32,4]{0,1:T(4,128)S(1)}, s32[32,4]{0,1:T(4,128)}, u32[]{:S(2)}) copy-start(s32[32,4]{0,1:T(4,128)} %param.12) | copy-start | bytes 1540
  19.4 42.5 %all-to-all-start = ((bf16[4,8,32,8,128]{4,3,1,0,2:T(8,128)(2,1)}), bf16[4,8,32,8,128]{4,3,1,0,2:T(8,128)(2,1)}, u32[]{:S(2)}, u32[]{:S(2)}) async-start(bf16[4,8,32,8,128]{4,3,1,0,2:T(8,128)(2,1)} %copy.202), calls=%async_computation | async-start | bytes 4194304 | tf_op jit(solution)/shard_map/all_to_all | solution.py:69
  30.9 2.7 %copy-start.5 = (bf16[96,8,8,128]{3,2,1,0:T(8,128)(2,1)}, bf16[96,8,8,128]{3,2,1,0:T(8,128)(2,1)S(1)}, u32[]{:S(2)}) copy-start(bf16[96,8,8,128]{3,2,1,0:T(8,128)(2,1)S(1)} %copy.207) | copy-start | bytes 4718596
  33.6 1.0 copy-start.3
  42.1 3.7 %copy-start.4 = (f32[8,8,32,96]{3,2,1,0:T(8,128)S(1)}, f32[8,8,32,96]{3,2,1,0:T(8,128)}, u32[]{:S(2)}) copy-start(f32[8,8,32,96]{3,2,1,0:T(8,128)} %copy-done.3) | copy-start | bytes 2359300
  42.2 3.7 %copy-start.7 = (bf16[96,8,8,128]{3,2,1,0:T(8,128)(2,1)S(1)}, bf16[96,8,8,128]{3,2,1,0:T(8,128)(2,1)}, u32[]{:S(2)}) copy-start(bf16[96,8,8,128]{3,2,1,0:T(8,128)(2,1)} %copy.208) | copy-start | bytes 4718596
  42.2 3.7 %copy-start.9 = (bf16[8,4,8,8,128]{4,3,2,1,0:T(8,128)(2,1)S(1)}, bf16[8,4,8,8,128]{4,3,2,1,0:T(8,128)(2,1)}, u32[]{:S(2)}) copy-start(bf16[8,4,8,8,128]{4,3,2,1,0:T(8,128)(2,1)} %copy-done.8) | copy-start | bytes 1572868
  45.9 1.9 %copy-start.13 = (bf16[8,4,8,8,128]{4,3,2,1,0:T(8,128)(2,1)S(1)}, bf16[8,4,8,8,128]{4,3,2,1,0:T(8,128)(2,1)}, u32[]{:S(2)}) copy-start(bf16[8,4,8,8,128]{4,3,2,1,0:T(8,128)(2,1)} %copy-done.12) | copy-start | bytes 1572868
  47.0 0.8 copy-start.10
  58.8 2.7 %copy-start.2 = (f32[2,8,96,1024]{3,2,1,0:T(8,128)}, f32[2,8,96,1024]{3,2,1,0:T(8,128)S(1)}, u32[]{:S(2)}) copy-start(f32[2,8,96,1024]{3,2,1,0:T(8,128)S(1)} %constant_dynamic-update-slice_fusion) | copy-start | bytes 18874372
  71.5 40.9 %all-to-all-start.1 = ((bf16[4,128,2,8,128]{4,3,2,0,1:T(8,128)(2,1)}), bf16[4,128,2,8,128]{4,3,2,0,1:T(8,128)(2,1)}, u32[]{:S(2)}, u32[]{:S(2)}) async-start(bf16[4,128,2,8,128]{4,3,2,0,1:T(8,128)(2,1)} %copy.164), calls=%async_computation.1 | async-start | bytes 4194304 | tf_op jit(solution)/shard_map/all_to_all | solution.py:74
  78.1 6.2 %copy-start.6 = (bf16[96,8,8,128]{3,2,1,0:T(8,128)(2,1)S(1)}, bf16[96,8,8,128]{3,2,1,0:T(8,128)(2,1)}, u32[]{:S(2)}) copy-start(bf16[96,8,8,128]{3,2,1,0:T(8,128)(2,1)} %copy-done.5) | copy-start | bytes 4718596
  78.1 6.2 %copy-start.11 = (bf16[8,8,32,96]{3,2,1,0:T(8,128)(2,1)S(1)}, bf16[8,8,32,96]{3,2,1,0:T(8,128)(2,1)}, u32[]{:S(2)}) copy-start(bf16[8,8,32,96]{3,2,1,0:T(8,128)(2,1)} %copy-done.10) | copy-start | bytes 1179652
  78.3 6.7 %copy-start.15 = (bf16[8,8,128,32]{2,3,1,0:T(8,128)(2,1)S(1)}, bf16[8,8,128,32]{2,3,1,0:T(8,128)(2,1)}, u32[]{:S(2)}) copy-start(bf16[8,8,128,32]{2,3,1,0:T(8,128)(2,1)} %get-tuple-element.34) | copy-start | bytes 1572868
  78.3 16.6 %collective-permute-start.2 = (bf16[2,8,32,1024]{3,2,1,0:T(8,128)(2,1)S(1)}, bf16[2,8,32,1024]{3,2,1,0:T(8,128)(2,1)S(1)}, u32[]{:S(2)}, u32[]{:S(2)}) collective-permute-start(bf16[2,8,32,1024]{3,2,1,0:T(8,128)(2,1)S(1)} %get-tuple-element.4), channel_id=1, source_target_pairs={{16,0},{32,16},{48,32},{64,48},{80,64},{96,80},{112,96},{128,112},... | collective-permute-start | bytes 3145736 | tf_op jit(solution)/shard_map/ppermute | solution.py:21
  80.4 15.4 %collective-permute-start.3 = (bf16[2,8,32,1024]{3,2,1,0:T(8,128)(2,1)S(1)}, bf16[2,8,32,1024]{3,2,1,0:T(8,128)(2,1)S(1)}, u32[]{:S(2)}, u32[]{:S(2)}) collective-permute-start(bf16[2,8,32,1024]{3,2,1,0:T(8,128)(2,1)S(1)} %get-tuple-element.5), channel_id=1, source_target_pairs={{0,16},{16,32},{32,48},{48,64},{64,80},{80,96},{96,112},{112,128},... | collective-permute-start | bytes 3145736 | tf_op jit(solution)/shard_map/ppermute | solution.py:21
  117.6 2.3 %copy-start.16 = (bf16[32,8,8,128]{3,1,2,0:T(8,128)(2,1)S(1)}, bf16[32,8,8,128]{3,1,2,0:T(8,128)(2,1)}, u32[]{:S(2)}) copy-start(bf16[32,8,8,128]{3,1,2,0:T(8,128)(2,1)} %copy.308) | copy-start | bytes 1572868
  126.5 2.1 %copy-start.1 = (bf16[8,32,2048]{2,1,0:T(8,128)(2,1)S(1)}, bf16[8,32,2048]{2,1,0:T(8,128)(2,1)}, u32[]{:S(2)}) copy-start(bf16[8,32,2048]{2,1,0:T(8,128)(2,1)} %param.10) | copy-start | bytes 3145732
